TPU v7x, 256 devices: a whole 4x4x8 slice. The times are simulated.
256 devices in a mesh: blk: 32 (over x, y, core), row: 8 (over z).
Axes of the slice: x: 4, y: 4, z: 8, core: 2. Of those that a mesh axis runs over, the one named last changes fastest.
Arguments:
- samples: bfloat16 [1024, 8192], P('blk', 'row'), may hold values from -8 to 8, as said below
- blocks: int32 [64, 4], replicated, may hold values from 0 to 31
- factor: float32 [64, 1024], P(None, 'row'), may hold values from -1.2 to 1.2
Outputs:
- cumulants: float32 [64, 1024, 1024], P('blk', 'row')
- factor_out: float32 [64, 1024], P(None, 'row')
Inputs may be any that keep to these rules, and one draw needn't show every extreme that they name: `samples`: channel values are drawn with mean zero.
All inputs are finite; a program needn't handle non-finite values.
Results may differ from a plain program's by a relative error of at most 0.0014.
Values may be sent and summed in bfloat16 or wider, within the bound.
No kernel may reach another device: no remote copies, remote signals or barrier semaphores. Data moves between devices by JAX's collectives and lax.ppermute only.
A program may use at most 64 MiB of HBM per device.

v0:
```python
import jax
import jax.numpy as jnp
from jax import lax
from jax.sharding import PartitionSpec as P

CHANNELS = 1024
BLOCK = 32
RANK = 64
SAMPLES = 8192
ITERS = 2


step_size = 0.2


def pair_rows(left, right):
    product = left[:, None, :].astype(jnp.float32) * right[None, :, :].astype(jnp.float32)
    return product.reshape(left.shape[0] * right.shape[0], left.shape[1]).astype(jnp.bfloat16)


def contract_last(left, right):
    return lax.dot_general(
        left, right, (((1,), (1,)), ((), ())), preferred_element_type=jnp.float32
    )


def gauss_terms(gram, count, width, row_lo):
    highest = lax.Precision.HIGHEST

    def part(first, second):
        return gram[first * width : (first + 1) * width, second * width : (second + 1) * width]

    cov_ab = lax.dynamic_slice_in_dim(part(0, 1), row_lo, count, 0)
    cov_ac = lax.dynamic_slice_in_dim(part(0, 2), row_lo, count, 0)
    cov_ad = lax.dynamic_slice_in_dim(part(0, 3), row_lo, count, 0)
    cov_cd = part(2, 3)
    cov_bd = part(1, 3)
    cov_bc = part(1, 2)
    first_term = cov_ab.reshape(-1)[:, None] * cov_cd.reshape(-1)[None, :]
    second_term = jnp.einsum("ik,jl->ijkl", cov_ac, cov_bd, precision=highest).reshape(
        count * width, width * width
    )
    third_term = jnp.einsum("il,jk->ijkl", cov_ad, cov_bc, precision=highest).reshape(
        count * width, width * width
    )
    return first_term + second_term + third_term


def add_cols(total, piece, start):
    old = lax.dynamic_slice_in_dim(total, start, piece.shape[1], 1)
    return lax.dynamic_update_slice_in_dim(total, old + piece, start, 1)


def add_grads(total, kslab, full, ids, row_lo, count, width):
    highest = lax.Precision.HIGHEST
    rank = full.shape[0]
    start_a = ids[0] * width + row_lo
    fac_a = lax.dynamic_slice_in_dim(full, start_a, count, 1)
    fac_b = lax.dynamic_slice_in_dim(full, ids[1] * width, width, 1)
    fac_c = lax.dynamic_slice_in_dim(full, ids[2] * width, width, 1)
    fac_d = lax.dynamic_slice_in_dim(full, ids[3] * width, width, 1)
    upair = (fac_a[:, :, None] * fac_b[:, None, :]).reshape(rank, count * width)
    vpair = (fac_c[:, :, None] * fac_d[:, None, :]).reshape(rank, width * width)
    model = lax.dot_general(upair, vpair, (((0,), (0,)), ((), ())), precision=highest)
    resid = kslab - model
    wmat = lax.dot_general(vpair, resid, (((1,), (1,)), ((), ())), precision=highest).reshape(
        rank, count, width
    )
    zmat = jnp.dot(upair, resid, precision=highest).reshape(rank, width, width)
    total = add_cols(total, jnp.sum(wmat * fac_b[:, None, :], axis=2), start_a)
    total = add_cols(total, jnp.sum(wmat * fac_a[:, :, None], axis=1), ids[1] * width)
    total = add_cols(total, jnp.sum(zmat * fac_d[:, None, :], axis=2), ids[2] * width)
    total = add_cols(total, jnp.sum(zmat * fac_c[:, :, None], axis=1), ids[3] * width)
    return total


def gather_factor(columns):
    return lax.all_gather(columns, "row", axis=1, tiled=True)


def per_device(samples, blocks, factor):
    width = BLOCK
    row_count = lax.axis_size("row")
    count = width // row_count
    row_lo = lax.axis_index("row") * count
    per_owner = blocks.shape[0] // lax.axis_size("blk")
    mine = lax.dynamic_slice_in_dim(blocks, lax.axis_index("blk") * per_owner, per_owner, 0)
    needed = mine.reshape(-1)
    pairs = width * width
    piece = lax.all_gather(samples, "blk", axis=0, tiled=True)
    pieces = piece.shape[0] // width
    owned = jnp.arange(pieces, dtype=jnp.int32)
    select = (needed[:, None] == owned[None, :]).astype(jnp.bfloat16)
    shaped = piece.reshape(pieces, width, piece.shape[1])
    taken = jnp.einsum("mb,bcs->mcs", select, shaped, preferred_element_type=jnp.float32)
    local = taken.astype(jnp.bfloat16)
    slabs = []
    whole = lax.all_gather(local, "row", axis=2, tiled=True)
    sample_block = min(SAMPLES, 2048)
    for slot in range(per_owner):
        source_a = whole[4 * slot]
        source_b = whole[4 * slot + 1]
        source_c = whole[4 * slot + 2]
        source_d = whole[4 * slot + 3]

        def accumulate(index, moment):
            low = index * sample_block
            left = lax.dynamic_slice(source_a, (row_lo, low), (count, sample_block))
            right = lax.dynamic_slice_in_dim(source_b, low, sample_block, 1)
            third = lax.dynamic_slice_in_dim(source_c, low, sample_block, 1)
            fourth = lax.dynamic_slice_in_dim(source_d, low, sample_block, 1)
            pmat = pair_rows(left, right)
            qmat = pair_rows(third, fourth)
            return moment + contract_last(pmat, qmat)

        moment = lax.fori_loop(
            0, SAMPLES // sample_block, accumulate, jnp.zeros((count * width, pairs), jnp.float32)
        )
        moment = moment / SAMPLES
        joined = whole[4 * slot : 4 * slot + 4].reshape(4 * width, whole.shape[2])
        gram = contract_last(joined, joined) / SAMPLES
        slabs.append(moment - gauss_terms(gram, count, width, row_lo))
    columns = factor
    full = gather_factor(columns)
    for step in range(ITERS):
        grad = jnp.zeros(full.shape, jnp.float32)
        for slot in range(per_owner):
            grad = add_grads(grad, slabs[slot], full, mine[slot], row_lo, count, width)
        owned_cols = lax.psum_scatter(grad, "row", scatter_dimension=1, tiled=True)
        owned_cols = lax.psum(owned_cols, "blk")
        squares = lax.psum(jnp.sum(owned_cols * owned_cols), "row")
        scale = lax.rsqrt(squares / (RANK * CHANNELS) + 1e-06)
        columns = columns + step_size * scale * owned_cols
        if step + 1 < ITERS:
            full = gather_factor(columns)
    return (jnp.stack(slabs), columns)


def solution(mesh):
    placed = (P("blk", "row"), P(), P(None, "row"))
    return jax.shard_map(
        per_device,
        mesh=mesh,
        in_specs=placed,
        out_specs=(P("blk", "row", None), P(None, "row")),
        check_vma=False,
    )
```

profile of v0, /device:TPU:32, one launch (start us, length us, event | category | flops | bytes accessed | tf_op | source)
XLA Modules:
  0.0 646.9 jit_solution(17991353607669108797)
XLA Ops:
  8.2 53.5 %all-gather.3.cloned.1.call-done = bf16[1024,1024]{1,0:T(8,128)(2,1)} async-done(((bf16[32,1024]{1,0:T(8,128)(2,1)}), bf16[1024,1024]{1,0:T(8,128)(2,1)}) %all-gather.3.cloned.1.call-update) | async-done | bytes 2097168 | tf_op jit(solution)/shard_map/all_gather | solution.py:90
  61.8 4.7 fusion.2
  72.3 26.5 %all_gather.14 = f32[64,1024]{1,0:T(8,128)S(1)} all-gather(f32[64,128]{1,0:T(8,128)S(1)} %copy-done.11), channel_id=1, replica_groups=mesh['blk'=32,'row'=8] {'row'}, dimensions={1}, use_global_device_ids=true | all-gather | bytes 294912 | tf_op jit(solution)/shard_map/all_gather | solution.py:78
  101.3 19.8 %all-gather.5.cloned.1.call-done = bf16[8,32,8192]{2,0,1:T(8,128)(2,1)} async-done(((bf16[8,32,1024]{2,0,1:T(8,128)(2,1)}), bf16[8,32,8192]{2,0,1:T(8,128)(2,1)}) %all-gather.5.cloned.1.call-update) | async-done | bytes 4194320 | tf_op jit(solution)/shard_map/all_gather | solution.py:98
  121.1 21.7 %fusion.10 = (bf16[1,32,8192]{2,0,1:T(2,128)(2,1)S(1)}, bf16[1,32,8192]{2,0,1:T(2,128)(2,1)}, bf16[1,32,8192]{2,0,1:T(2,128)(2,1)}, bf16[1,32,8192]{2,0,1:T(2,12...) fusion(bf16[8,32,8192]{2,0,1:T(8,128)(2,1)} %all-gather.5.clone, ...), kind=kLoop, calls=%fused_computation.112 | loop fusion | bytes 8388608 | tf_op jit(solution)/shard_map/slice | solution.py:104
  142.8 2.0 copy_bitcast_fusion.6
  144.8 1.1 copy_bitcast_fusion.4
  145.9 31.4 %while.32 = (s32[]{:T(128)}, f32[128,1024]{1,0:T(8,128)S(1)}, bf16[32,8192]{1,0:T(8,128)(2,1)}, s32[]{:T(128)}, bf16[32,8192]{1,0:T(8,128)(2,1)S(1)}, /*index=5*...) while((s32[]{:T(128)}, f32[128,1024]{1,0:T(8,128)S(1)}, ...), condition=%wide.region_1.0_spmd.clone, body=%wide.region_0.0_spmd.clone.sunk | while | flops 542056448 | bytes 12533941 | solution.py:116
  146.0 3.0 multiply_convert_fusion.9
  150.0 3.8 convolution_add_fusion.4
  153.9 3.0 multiply_convert_fusion.9
  157.9 3.8 convolution_add_fusion.4
  161.7 3.0 multiply_convert_fusion.9
  165.7 3.8 convolution_add_fusion.4
  169.6 3.0 multiply_convert_fusion.9
  173.6 3.8 convolution_add_fusion.4
  177.4 6.7 %fusion.11 = (bf16[4,32,8192]{2,0,1:T(4,128)(2,1)S(1)}, bf16[4,32,8192]{2,0,1:T(4,128)(2,1)}) fusion(bf16[8,32,8192]{2,0,1:T(8,128)(2,1)} %all-gather.5.cloned.1.call-done), kind=kLoop, calls=%fused_computation.113 | loop fusion | bytes 8388608 | tf_op jit(solution)/shard_map/slice | solution.py:120
  184.0 1.2 copy.68
  186.9 1.8 reshape.324
  188.7 2.7 copy.69
  192.6 1.8 reshape.325
  194.5 1.4 add_subtract_fusion.1
  196.5 1.0 copy.75
  197.6 3.6 copy_bitcast_fusion.2
  201.1 2.1 copy_bitcast_fusion
  203.3 35.3 %while.33 = (s32[]{:T(128)}, f32[128,1024]{1,0:T(8,128)S(1)}, bf16[32,8192]{1,0:T(8,128)(2,1)}, s32[]{:T(128)}, bf16[32,8192]{1,0:T(8,128)(2,1)S(1)}, /*index=5*...) while((s32[]{:T(128)}, f32[128,1024]{1,0:T(8,128)S(1)}, ...), condition=%wide.region_3.0_spmd.clone, body=%wide.region_2.0_spmd.clone.sunk | while | flops 542056448 | bytes 12533941 | solution.py:116
  204.3 3.0 multiply_convert_fusion.11
  208.2 3.8 convolution_add_fusion.5
  213.0 3.0 multiply_convert_fusion.11
  217.0 3.8 convolution_add_fusion.5
  221.8 3.0 multiply_convert_fusion.11
  225.8 3.8 convolution_add_fusion.5
  230.6 3.0 multiply_convert_fusion.11
  234.6 3.8 convolution_add_fusion.5
  238.9 1.8 reshape.327
  241.0 1.8 reshape.328
  242.9 1.4 add_subtract_fusion
  245.9 1.7 multiply_reduce_fusion.6
  250.8 37.1 %reduce-scatter.3.cloned.1.call-done = f32[64,128]{0,1:T(8,128)} async-done(((f32[64,1024]{0,1:T(8,128)}), f32[64,128]{0,1:T(8,128)}) %reduce-scatter.3.cloned.1.call-update) | async-done | bytes 32784 | tf_op jit(solution)/shard_map/reduce_scatter | solution.py:129
  287.9 124.3 %psum.28 = f32[64,128]{0,1:T(8,128)S(1)} all-reduce(f32[64,128]{0,1:T(8,128)} %reduce-scatter.3.cloned.1.call-done), channel_id=1, replica_groups=mesh['blk'=32,'row'=8] {'blk'}, use_global_device_ids=true, to_apply=%region_13.0 | all-reduce | flops 8192 | bytes 65536 | tf_op jit(solution)/shard_map/psum | solution.py:130
  412.9 16.0 %psum.29 = f32[]{:T(128)} all-reduce(f32[]{:T(128)} %multiply_reduce_fusion.13), channel_id=1, replica_groups=mesh['blk'=32,'row'=8] {'row'}, use_global_device_ids=true, to_apply=%region_15.0 | all-reduce | flops 1 | bytes 8 | tf_op jit(solution)/shard_map/psum | solution.py:131
  429.7 24.3 %all_gather.15 = f32[64,1024]{0,1:T(8,128)S(1)} all-gather(f32[64,128]{0,1:T(8,128)S(1)} %multiply_add_fusion.1), channel_id=1, replica_groups=mesh['blk'=32,'row'=8] {'row'}, dimensions={1}, use_global_device_ids=true | all-gather | bytes 294912 | tf_op jit(solution)/shard_map/all_gather | solution.py:78
  457.3 1.7 multiply_reduce_fusion
  459.7 1.7 multiply_reduce_fusion.2
  463.1 34.0 %reduce-scatter.5.cloned.1.call-done = f32[64,128]{0,1:T(8,128)} async-done(((f32[64,1024]{0,1:T(8,128)}), f32[64,128]{0,1:T(8,128)}) %reduce-scatter.5.cloned.1.call-update) | async-done | bytes 32784 | tf_op jit(solution)/shard_map/reduce_scatter | solution.py:129
  497.1 124.3 %psum.30 = f32[64,128]{0,1:T(8,128)S(1)} all-reduce(f32[64,128]{0,1:T(8,128)} %reduce-scatter.5.cloned.1.call-done), channel_id=1, replica_groups=mesh['blk'=32,'row'=8] {'blk'}, use_global_device_ids=true, to_apply=%region_25.0 | all-reduce | flops 8192 | bytes 65536 | tf_op jit(solution)/shard_map/psum | solution.py:130
  622.0 1.0 pad_maximum_fusion
  623.1 15.9 %psum.31 = f32[]{:T(128)} all-reduce(f32[]{:T(128)} %multiply_reduce_fusion.8), channel_id=1, replica_groups=mesh['blk'=32,'row'=8] {'row'}, use_global_device_ids=true, to_apply=%region_27.0 | all-reduce | flops 1 | bytes 8 | tf_op jit(solution)/shard_map/psum | solution.py:131
  (143 shorter events, 32.7 us)
Async XLA Ops:
  7.2 0.8 copy-start
  7.2 65.1 %copy-start.11 = (f32[64,128]{1,0:T(8,128)S(1)}, f32[64,128]{1,0:T(8,128)}, u32[]{:S(2)}) copy-start(f32[64,128]{1,0:T(8,128)} %param.9) | copy-start | bytes 98308
  7.2 54.6 %all-gather.3.cloned.1.call-start = ((), (), s32[]{:S(2)}) async-start(), calls=%async_computation.2 | async-start | bytes 2162688 | tf_op jit(solution)/shard_map/all_gather | solution.py:90
  7.9 113.2 %all-gather.5.cloned.1.call-start = ((), (), s32[]{:S(2)}) async-start(), calls=%async_computation.3 | async-start | bytes 4718592 | tf_op jit(solution)/shard_map/all_gather | solution.py:98
  66.5 221.4 %reduce-scatter.3.cloned.1.call-start = ((), (), s32[]{:S(2)}) async-start(), calls=%async_computation.4 | async-start | bytes 589824 | tf_op jit(solution)/shard_map/reduce_scatter | solution.py:129
  192.3 2.1 copy-start.12
  194.4 1.5 copy-start.2
  196.5 4.6 copy-start.4
  196.5 4.6 copy-start.6
  197.6 3.6 copy-start.7
  242.8 1.5 copy-start.1
  244.3 3.4 copy-start.3
  244.3 3.4 copy-start.5
  245.9 3.3 copy-start.10
  249.9 0.8 copy-start.9
  250.7 246.3 %reduce-scatter.5.cloned.1.call-start = ((), (), s32[]{:S(2)}) async-start(), calls=%async_computation.5 | async-start | bytes 589824 | tf_op jit(solution)/shard_map/reduce_scatter | solution.py:129
  462.3 0.8 copy-start.8
Sparse Core Ops, SparseCore 0:
  10.6 51.1 all-gather.2
  66.6 54.4 all-gather.4
  250.8 36.9 reduce-scatter.2
  463.2 33.8 reduce-scatter.4
where the time goes:
time: 648 us; the launch traced here: 647 us
  blocking collectives  331 us (51%)
  waiting for transfers between devices  145 us (22%)
  local copies, waits for them, and re-layouts  57.5 us (9%)
  matrix products  47.2 us (7%)
  other arithmetic  44.2 us (7%)
  between operations  20.7 us (3%)
    psum x2, blocking collectives, per_device(): owned_cols = lax.psum(owned_cols, 'blk')  249 us
    reduce_scatter x2, waiting for transfers between devices, per_device(): owned_cols = lax.psum_scatter(grad, 'row', scatter_dimension=1, tiled=True)  71.1 us
    all_gather x1, waiting for transfers between devices, per_device(): piece = lax.all_gather(samples, 'blk', axis=0, tiled=True)  53.5 us
    all_gather x2, blocking collectives, gather_factor(): return lax.all_gather(columns, 'row', axis=1, tiled=True)  50.7 us
    psum x2, blocking collectives, per_device(): squares = lax.psum(jnp.sum(owned_cols * owned_cols), 'row')  32 us
    dot_general x10, matrix products, contract_last(): lax.dot_general(left, right, (((1,), (1,)), ((), ())), preferred_element_...  31.6 us
    convert_element_type x16, other arithmetic, pair_rows(): product.reshape(left.shape[0] * right.shape[0], left.shape[1])  24.8 us
    slice x1, local copies, waits for them, and re-layouts, per_device(): source_d = whole[4 * slot + 3]  21.7 us
  transfers between devices with their start and end apart: 4, of which 4 were waited for; matrix products, arithmetic and copies ran while one was open for 1% of the time, Pallas kernels for 0%

commit v1 on v0

--- a/solution.py
+++ b/solution.py
@@ -78,6 +78,17 @@
     return lax.all_gather(columns, "row", axis=1, tiled=True)
 
 
+def all_sum(value):
+    for axis in ("row", "blk"):
+        size = lax.axis_size(axis)
+        stride = 1
+        while stride < size:
+            pairs = [(index, index ^ stride) for index in range(size)]
+            value = value + lax.ppermute(value, axis, pairs)
+            stride *= 2
+    return value
+
+
 def per_device(samples, blocks, factor):
     width = BLOCK
     row_count = lax.axis_size("row")
@@ -120,19 +131,16 @@
         joined = whole[4 * slot : 4 * slot + 4].reshape(4 * width, whole.shape[2])
         gram = contract_last(joined, joined) / SAMPLES
         slabs.append(moment - gauss_terms(gram, count, width, row_lo))
-    columns = factor
-    full = gather_factor(columns)
+    full = gather_factor(factor)
     for step in range(ITERS):
         grad = jnp.zeros(full.shape, jnp.float32)
         for slot in range(per_owner):
             grad = add_grads(grad, slabs[slot], full, mine[slot], row_lo, count, width)
-        owned_cols = lax.psum_scatter(grad, "row", scatter_dimension=1, tiled=True)
-        owned_cols = lax.psum(owned_cols, "blk")
-        squares = lax.psum(jnp.sum(owned_cols * owned_cols), "row")
-        scale = lax.rsqrt(squares / (RANK * CHANNELS) + 1e-06)
-        columns = columns + step_size * scale * owned_cols
-        if step + 1 < ITERS:
-            full = gather_factor(columns)
+        grad = all_sum(grad)
+        scale = lax.rsqrt(jnp.mean(grad * grad) + 1e-06)
+        full = full + step_size * scale * grad
+    col_count = factor.shape[1]
+    columns = lax.dynamic_slice_in_dim(full, lax.axis_index("row") * col_count, col_count, 1)
     return (jnp.stack(slabs), columns)
 
 

time: 648 us -> 524 us (0.81)
  the two profiles are of different devices: /device:TPU:32 before, /device:TPU:6 now
where the time goes in v1:
time: 524 us; the launch traced here: 516 us
  waiting for transfers between devices  294 us (56%)
  local copies, waits for them, and re-layouts  55.2 us (11%)
  matrix products  47.1 us (9%)
  other arithmetic  45.6 us (9%)
  blocking collectives  29.3 us (6%)
  starting transfers between devices  21.7 us (4%)
  between operations  21.7 us (4%)
    ppermute x16, waiting for transfers between devices, all_sum(): value = value + lax.ppermute(value, axis, pairs)  218 us
    all_gather x1, waiting for transfers between devices, per_device(): piece = lax.all_gather(samples, 'blk', axis=0, tiled=True)  53.5 us
    dot_general x10, matrix products, contract_last(): lax.dot_general(left, right, (((1,), (1,)), ((), ())), preferred_element_...  31.6 us
    all_gather x1, blocking collectives, gather_factor(): return lax.all_gather(columns, 'row', axis=1, tiled=True)  29.3 us
    convert_element_type x16, other arithmetic, pair_rows(): product.reshape(left.shape[0] * right.shape[0], left.shape[1])  24.9 us
    slice x1, local copies, waits for them, and re-layouts, per_device(): source_d = whole[4 * slot + 3]  21.7 us
    ppermute x16, starting transfers between devices, all_sum(): value = value + lax.ppermute(value, axis, pairs)  21.6 us
    all_gather x1, waiting for transfers between devices, per_device(): whole = lax.all_gather(local, 'row', axis=2, tiled=True)  21.5 us
  transfers between devices with their start and end apart: 18, of which 18 were waited for; matrix products, arithmetic and copies ran while one was open for 1% of the time, Pallas kernels for 0%

profile of v1, /device:TPU:6, one launch (start us, length us, event | category | flops | bytes accessed | tf_op | source)
XLA Modules:
  0.0 515.5 jit_solution(10120741911777920129)
XLA Ops:
  8.2 53.5 %all-gather.3.cloned.1.call-done = bf16[1024,1024]{1,0:T(8,128)(2,1)} async-done(((bf16[32,1024]{1,0:T(8,128)(2,1)}), bf16[1024,1024]{1,0:T(8,128)(2,1)}) %all-gather.3.cloned.1.call-update) | async-done | bytes 2097168 | tf_op jit(solution)/shard_map/all_gather | solution.py:101
  61.7 4.7 fusion.2
  72.4 29.3 %all_gather.11 = f32[64,1024]{0,1:T(8,128)S(1)} all-gather(f32[64,128]{0,1:T(8,128)S(1)} %copy.70), channel_id=1, replica_groups=mesh['blk'=32,'row'=8] {'row'}, dimensions={1}, use_global_device_ids=true | all-gather | bytes 294912 | tf_op jit(solution)/shard_map/all_gather | solution.py:78
  103.8 21.5 %all-gather.5.cloned.1.call-done = bf16[8,32,8192]{2,0,1:T(8,128)(2,1)} async-done(((bf16[8,32,1024]{2,0,1:T(8,128)(2,1)}), bf16[8,32,8192]{2,0,1:T(8,128)(2,1)}) %all-gather.5.cloned.1.call-update) | async-done | bytes 4194320 | tf_op jit(solution)/shard_map/all_gather | solution.py:109
  125.3 21.7 %fusion.10 = (bf16[1,32,8192]{2,0,1:T(2,128)(2,1)S(1)}, bf16[1,32,8192]{2,0,1:T(2,128)(2,1)}, bf16[1,32,8192]{2,0,1:T(2,128)(2,1)}, bf16[1,32,8192]{2,0,1:T(2,12...) fusion(bf16[8,32,8192]{2,0,1:T(8,128)(2,1)} %all-gather.5.clone, ...), kind=kLoop, calls=%fused_computation.113 | loop fusion | bytes 8388608 | tf_op jit(solution)/shard_map/slice | solution.py:115
  147.0 1.9 copy_bitcast_fusion.6
  150.1 31.4 %while.32 = (s32[]{:T(128)}, f32[128,1024]{1,0:T(8,128)S(1)}, bf16[32,8192]{1,0:T(8,128)(2,1)}, s32[]{:T(128)}, bf16[32,8192]{1,0:T(8,128)(2,1)S(1)}, /*index=5*...) while((s32[]{:T(128)}, f32[128,1024]{1,0:T(8,128)S(1)}, ...), condition=%wide.region_1.0_spmd.clone, body=%wide.region_0.0_spmd.clone.sunk | while | flops 542056448 | bytes 12533941 | solution.py:127
  150.2 3.0 multiply_convert_fusion.9
  154.2 3.8 convolution_add_fusion.4
  158.0 3.0 multiply_convert_fusion.9
  162.0 3.8 convolution_add_fusion.4
  165.9 3.0 multiply_convert_fusion.9
  169.9 3.8 convolution_add_fusion.4
  173.7 3.0 multiply_convert_fusion.9
  177.7 3.8 convolution_add_fusion.4
  181.5 6.6 %fusion.11 = (bf16[4,32,8192]{2,0,1:T(4,128)(2,1)S(1)}, bf16[4,32,8192]{2,0,1:T(4,128)(2,1)}) fusion(bf16[8,32,8192]{2,0,1:T(8,128)(2,1)} %all-gather.5.cloned.1.call-done), kind=kLoop, calls=%fused_computation.114 | loop fusion | bytes 8388608 | tf_op jit(solution)/shard_map/slice | solution.py:131
  192.2 2.7 copy.69
  201.0 3.6 copy_bitcast_fusion.2
  204.6 2.1 copy_bitcast_fusion
  206.7 35.4 %while.33 = (s32[]{:T(128)}, f32[128,1024]{1,0:T(8,128)S(1)}, bf16[32,8192]{1,0:T(8,128)(2,1)}, s32[]{:T(128)}, bf16[32,8192]{1,0:T(8,128)(2,1)S(1)}, /*index=5*...) while((s32[]{:T(128)}, f32[128,1024]{1,0:T(8,128)S(1)}, ...), condition=%wide.region_3.0_spmd.clone, body=%wide.region_2.0_spmd.clone.sunk | while | flops 542056448 | bytes 12533941 | solution.py:127
  207.7 3.0 multiply_convert_fusion.11
  211.7 3.8 convolution_add_fusion.5
  216.5 3.0 multiply_convert_fusion.11
  220.5 3.8 convolution_add_fusion.5
  225.3 3.0 multiply_convert_fusion.11
  229.3 3.8 convolution_add_fusion.5
  234.1 3.0 multiply_convert_fusion.11
  238.1 3.8 convolution_add_fusion.5
  253.5 13.7 %collective-permute-done = f32[64,1024]{0,1:T(8,128)S(1)} collective-permute-done((f32[64,1024]{0,1:T(8,128)S(1)}, f32[64,1024]{0,1:T(8,128)S(1)}, u32[]{:S(2)}, u32[]{:S(2)}) %collective-permute-start) | collective-permute-done | bytes 262176 | tf_op jit(solution)/shard_map/ppermute | solution.py:87
  269.2 23.2 %collective-permute-done.1 = f32[64,1024]{0,1:T(8,128)S(1)} collective-permute-done((f32[64,1024]{0,1:T(8,128)S(1)}, f32[64,1024]{0,1:T(8,128)S(1)}, u32[]{:S(2)}, u32[]{:S(2)}) %collective-permute-start.1) | collective-permute-done | bytes 262176 | tf_op jit(solution)/shard_map/ppermute | solution.py:87
  292.4 2.9 collective-permute-start.2
  295.3 24.5 %collective-permute-done.2 = f32[64,1024]{0,1:T(8,128)S(1)} collective-permute-done((f32[64,1024]{0,1:T(8,128)S(1)}, f32[64,1024]{0,1:T(8,128)S(1)}, u32[]{:S(2)}, u32[]{:S(2)}) %collective-permute-start.2) | collective-permute-done | bytes 262176 | tf_op jit(solution)/shard_map/ppermute | solution.py:87
  320.0 1.9 collective-permute-done.3
  322.8 13.2 %collective-permute-done.4 = f32[64,1024]{0,1:T(8,128)S(1)} collective-permute-done((f32[64,1024]{0,1:T(8,128)S(1)}, f32[64,1024]{0,1:T(8,128)S(1)}, u32[]{:S(2)}, u32[]{:S(2)}) %collective-permute-start.4) | collective-permute-done | bytes 262176 | tf_op jit(solution)/shard_map/ppermute | solution.py:87
  336.1 2.7 collective-permute-start.5
  338.8 12.0 %collective-permute-done.5 = f32[64,1024]{0,1:T(8,128)S(1)} collective-permute-done((f32[64,1024]{0,1:T(8,128)S(1)}, f32[64,1024]{0,1:T(8,128)S(1)}, u32[]{:S(2)}, u32[]{:S(2)}) %collective-permute-start.5) | collective-permute-done | bytes 262176 | tf_op jit(solution)/shard_map/ppermute | solution.py:87
  352.3 10.9 %collective-permute-done.6 = f32[64,1024]{0,1:T(8,128)S(1)} collective-permute-done((f32[64,1024]{0,1:T(8,128)S(1)}, f32[64,1024]{0,1:T(8,128)S(1)}, u32[]{:S(2)}, u32[]{:S(2)}) %collective-permute-start.6) | collective-permute-done | bytes 262176 | tf_op jit(solution)/shard_map/ppermute | solution.py:87
  365.1 11.4 %collective-permute-done.7 = f32[64,1024]{0,1:T(8,128)S(1)} collective-permute-done((f32[64,1024]{0,1:T(8,128)S(1)}, f32[64,1024]{0,1:T(8,128)S(1)}, u32[]{:S(2)}, u32[]{:S(2)}) %collective-permute-start.7) | collective-permute-done | bytes 262176 | tf_op jit(solution)/shard_map/ppermute | solution.py:87
  386.5 11.0 %collective-permute-done.8 = f32[64,1024]{0,1:T(8,128)S(1)} collective-permute-done((f32[64,1024]{0,1:T(8,128)S(1)}, f32[64,1024]{0,1:T(8,128)S(1)}, u32[]{:S(2)}, u32[]{:S(2)}) %collective-permute-start.8) | collective-permute-done | bytes 262176 | tf_op jit(solution)/shard_map/ppermute | solution.py:87
  399.2 19.7 %collective-permute-done.9 = f32[64,1024]{0,1:T(8,128)S(1)} collective-permute-done((f32[64,1024]{0,1:T(8,128)S(1)}, f32[64,1024]{0,1:T(8,128)S(1)}, u32[]{:S(2)}, u32[]{:S(2)}) %collective-permute-start.9) | collective-permute-done | bytes 262176 | tf_op jit(solution)/shard_map/ppermute | solution.py:87
  419.0 3.5 collective-permute-start.10
  422.5 24.6 %collective-permute-done.10 = f32[64,1024]{0,1:T(8,128)S(1)} collective-permute-done((f32[64,1024]{0,1:T(8,128)S(1)}, f32[64,1024]{0,1:T(8,128)S(1)}, u32[]{:S(2)}, u32[]{:S(2)}) %collective-permute-start.10) | collective-permute-done | bytes 262176 | tf_op jit(solution)/shard_map/ppermute | solution.py:87
  447.2 1.9 collective-permute-done.11
  449.3 13.9 %collective-permute-done.12 = f32[64,1024]{0,1:T(8,128)S(1)} collective-permute-done((f32[64,1024]{0,1:T(8,128)S(1)}, f32[64,1024]{0,1:T(8,128)S(1)}, u32[]{:S(2)}, u32[]{:S(2)}) %collective-permute-start.12) | collective-permute-done | bytes 262176 | tf_op jit(solution)/shard_map/ppermute | solution.py:87
  463.3 3.7 collective-permute-start.13
  467.0 11.6 %collective-permute-done.13 = f32[64,1024]{0,1:T(8,128)S(1)} collective-permute-done((f32[64,1024]{0,1:T(8,128)S(1)}, f32[64,1024]{0,1:T(8,128)S(1)}, u32[]{:S(2)}, u32[]{:S(2)}) %collective-permute-start.13) | collective-permute-done | bytes 262176 | tf_op jit(solution)/shard_map/ppermute | solution.py:87
  479.4 13.1 %collective-permute-done.14 = f32[64,1024]{0,1:T(8,128)S(1)} collective-permute-done((f32[64,1024]{0,1:T(8,128)S(1)}, f32[64,1024]{0,1:T(8,128)S(1)}, u32[]{:S(2)}, u32[]{:S(2)}) %collective-permute-start.14) | collective-permute-done | bytes 262176 | tf_op jit(solution)/shard_map/ppermute | solution.py:87
  493.7 11.5 %collective-permute-done.15 = f32[64,1024]{0,1:T(8,128)S(1)} collective-permute-done((f32[64,1024]{0,1:T(8,128)S(1)}, f32[64,1024]{0,1:T(8,128)S(1)}, u32[]{:S(2)}, u32[]{:S(2)}) %collective-permute-start.15) | collective-permute-done | bytes 262176 | tf_op jit(solution)/shard_map/ppermute | solution.py:87
  (170 shorter events, 59.8 us)
Async XLA Ops:
  7.2 0.8 copy-start
  7.2 65.1 %copy-start.13 = (f32[64,128]{1,0:T(8,128)S(1)}, f32[64,128]{1,0:T(8,128)}, u32[]{:S(2)}) copy-start(f32[64,128]{1,0:T(8,128)} %param.9) | copy-start | bytes 98308
  7.2 54.5 %all-gather.3.cloned.1.call-start = ((), (), s32[]{:S(2)}) async-start(), calls=%async_computation | async-start | bytes 2162688 | tf_op jit(solution)/shard_map/all_gather | solution.py:101
  7.9 117.4 %all-gather.5.cloned.1.call-start = ((), (), s32[]{:S(2)}) async-start(), calls=%async_computation.1 | async-start | bytes 4718592 | tf_op jit(solution)/shard_map/all_gather | solution.py:109
  101.8 0.8 copy-start.9
  197.8 1.5 copy-start.3
  200.0 4.6 copy-start.5
  200.0 4.6 copy-start.7
  201.0 3.6 copy-start.8
  246.3 1.5 copy-start.2
  247.8 3.4 copy-start.4
  247.8 3.4 copy-start.6
  249.4 3.3 copy-start.11
  253.4 13.8 %collective-permute-start = (f32[64,1024]{0,1:T(8,128)S(1)}, f32[64,1024]{0,1:T(8,128)S(1)}, u32[]{:S(2)}, u32[]{:S(2)}) collective-permute-start(f32[64,1024]{0,1:T(8,128)S(1)} %add_dynamic-update-slice_fusion.6), channel_id=1, source_target_pairs={{0,1},{1,0},{2,3},{3,2},{4,5},{5,4},{6,7},{7,6},{8,9},{9,8},{10,11... | collective-permute-start | bytes 786440 | tf_op jit(solution)/shard_map/ppermute | solution.py:87
  267.3 25.1 %collective-permute-start.1 = (f32[64,1024]{0,1:T(8,128)S(1)}, f32[64,1024]{0,1:T(8,128)S(1)}, u32[]{:S(2)}, u32[]{:S(2)}) collective-permute-start(f32[64,1024]{0,1:T(8,128)S(1)} %add.315), channel_id=1, source_target_pairs={{0,2},{1,3},{2,0},{3,1},{4,6},{5,7},{6,4},{7,5},{8,10},{9,11},{10,... | collective-permute-start | bytes 786440 | tf_op jit(solution)/shard_map/ppermute | solution.py:87
  292.4 27.4 %collective-permute-start.2 = (f32[64,1024]{0,1:T(8,128)S(1)}, f32[64,1024]{0,1:T(8,128)S(1)}, u32[]{:S(2)}, u32[]{:S(2)}) collective-permute-start(f32[64,1024]{0,1:T(8,128)S(1)} %add.316), channel_id=1, source_target_pairs={{0,4},{1,5},{2,6},{3,7},{4,0},{5,1},{6,2},{7,3},{8,12},{9,13},{10,... | collective-permute-start | bytes 786440 | tf_op jit(solution)/shard_map/ppermute | solution.py:87
  319.9 2.0 collective-permute-start.3
  322.0 14.1 %collective-permute-start.4 = (f32[64,1024]{0,1:T(8,128)S(1)}, f32[64,1024]{0,1:T(8,128)S(1)}, u32[]{:S(2)}, u32[]{:S(2)}) collective-permute-start(f32[64,1024]{0,1:T(8,128)S(1)} %add.318), channel_id=1, source_target_pairs={{0,16},{8,24},{16,0},{24,8},{32,48},{40,56},{48,32},{56,40},{64,80... | collective-permute-start | bytes 786440 | tf_op jit(solution)/shard_map/ppermute | solution.py:87
  336.1 41.8 %copy-start.10 = (f32[64,1024]{0,1:T(8,128)S(1)}, f32[64,1024]{0,1:T(8,128)}, u32[]{:S(2)}) copy-start(f32[64,1024]{0,1:T(8,128)} %copy-done.9) | copy-start | bytes 786436
  336.1 14.7 %collective-permute-start.5 = (f32[64,1024]{0,1:T(8,128)S(1)}, f32[64,1024]{0,1:T(8,128)S(1)}, u32[]{:S(2)}, u32[]{:S(2)}) collective-permute-start(f32[64,1024]{0,1:T(8,128)S(1)} %add.319), channel_id=1, source_target_pairs={{0,32},{8,40},{16,48},{24,56},{32,0},{40,8},{48,16},{56,24},{64,96... | collective-permute-start | bytes 786440 | tf_op jit(solution)/shard_map/ppermute | solution.py:87
  350.9 12.3 %collective-permute-start.6 = (f32[64,1024]{0,1:T(8,128)S(1)}, f32[64,1024]{0,1:T(8,128)S(1)}, u32[]{:S(2)}, u32[]{:S(2)}) collective-permute-start(f32[64,1024]{0,1:T(8,128)S(1)} %add.320), channel_id=1, source_target_pairs={{0,64},{8,72},{16,80},{24,88},{32,96},{40,104},{48,112},{56,120},{... | collective-permute-start | bytes 786440 | tf_op jit(solution)/shard_map/ppermute | solution.py:87
  363.3 13.2 %collective-permute-start.7 = (f32[64,1024]{0,1:T(8,128)S(1)}, f32[64,1024]{0,1:T(8,128)S(1)}, u32[]{:S(2)}, u32[]{:S(2)}) collective-permute-start(f32[64,1024]{0,1:T(8,128)S(1)} %add.321), channel_id=1, source_target_pairs={{0,128},{8,136},{16,144},{24,152},{32,160},{40,168},{48,176},{56,1... | collective-permute-start | bytes 786440 | tf_op jit(solution)/shard_map/ppermute | solution.py:87
  378.0 1.8 copy-start.12
  386.4 11.1 %collective-permute-start.8 = (f32[64,1024]{0,1:T(8,128)S(1)}, f32[64,1024]{0,1:T(8,128)S(1)}, u32[]{:S(2)}, u32[]{:S(2)}) collective-permute-start(f32[64,1024]{0,1:T(8,128)S(1)} %add_dynamic-update-slice_fusion), channel_id=1, source_target_pairs={{0,1},{1,0},{2,3},{3,2},{4,5},{5,4},{6,7},{7,6},{8,9},{9,8},{10,11... | collective-permute-start | bytes 786440 | tf_op jit(solution)/shard_map/ppermute | solution.py:87
  397.6 21.4 %collective-permute-start.9 = (f32[64,1024]{0,1:T(8,128)S(1)}, f32[64,1024]{0,1:T(8,128)S(1)}, u32[]{:S(2)}, u32[]{:S(2)}) collective-permute-start(f32[64,1024]{0,1:T(8,128)S(1)} %add.332), channel_id=1, source_target_pairs={{0,2},{1,3},{2,0},{3,1},{4,6},{5,7},{6,4},{7,5},{8,10},{9,11},{10,... | collective-permute-start | bytes 786440 | tf_op jit(solution)/shard_map/ppermute | solution.py:87
  419.0 28.1 %collective-permute-start.10 = (f32[64,1024]{0,1:T(8,128)S(1)}, f32[64,1024]{0,1:T(8,128)S(1)}, u32[]{:S(2)}, u32[]{:S(2)}) collective-permute-start(f32[64,1024]{0,1:T(8,128)S(1)} %add.333), channel_id=1, source_target_pairs={{0,4},{1,5},{2,6},{3,7},{4,0},{5,1},{6,2},{7,3},{8,12},{9,13},{10,... | collective-permute-start | bytes 786440 | tf_op jit(solution)/shard_map/ppermute | solution.py:87
  447.1 2.0 collective-permute-start.11
  449.2 14.1 %collective-permute-start.12 = (f32[64,1024]{0,1:T(8,128)S(1)}, f32[64,1024]{0,1:T(8,128)S(1)}, u32[]{:S(2)}, u32[]{:S(2)}) collective-permute-start(f32[64,1024]{0,1:T(8,128)S(1)} %add.335), channel_id=1, source_target_pairs={{0,16},{8,24},{16,0},{24,8},{32,48},{40,56},{48,32},{56,40},{64,80... | collective-permute-start | bytes 786440 | tf_op jit(solution)/shard_map/ppermute | solution.py:87
  463.3 15.4 %collective-permute-start.13 = (f32[64,1024]{0,1:T(8,128)S(1)}, f32[64,1024]{0,1:T(8,128)S(1)}, u32[]{:S(2)}, u32[]{:S(2)}) collective-permute-start(f32[64,1024]{0,1:T(8,128)S(1)} %add.336), channel_id=1, source_target_pairs={{0,32},{8,40},{16,48},{24,56},{32,0},{40,8},{48,16},{56,24},{64,96... | collective-permute-start | bytes 786440 | tf_op jit(solution)/shard_map/ppermute | solution.py:87
  478.7 13.8 %collective-permute-start.14 = (f32[64,1024]{0,1:T(8,128)S(1)}, f32[64,1024]{0,1:T(8,128)S(1)}, u32[]{:S(2)}, u32[]{:S(2)}) collective-permute-start(f32[64,1024]{0,1:T(8,128)S(1)} %add.337), channel_id=1, source_target_pairs={{0,64},{8,72},{16,80},{24,88},{32,96},{40,104},{48,112},{56,120},{... | collective-permute-start | bytes 786440 | tf_op jit(solution)/shard_map/ppermute | solution.py:87
  492.5 15.7 %copy-start.1 = (s32[64,4]{0,1:T(4,128)S(1)}, s32[64,4]{0,1:T(4,128)}, u32[]{:S(2)}) copy-start(s32[64,4]{0,1:T(4,128)} %param.8) | copy-start | bytes 3076
  492.6 12.7 %collective-permute-start.15 = (f32[64,1024]{0,1:T(8,128)S(1)}, f32[64,1024]{0,1:T(8,128)S(1)}, u32[]{:S(2)}, u32[]{:S(2)}) collective-permute-start(f32[64,1024]{0,1:T(8,128)S(1)} %add.338), channel_id=1, source_target_pairs={{0,128},{8,136},{16,144},{24,152},{32,160},{40,168},{48,176},{56,1... | collective-permute-start | bytes 786440 | tf_op jit(solution)/shard_map/ppermute | solution.py:87
Sparse Core Ops, SparseCore 0:
  10.6 51.1 all-gather.2
  66.6 58.6 all-gather.4
